TPU v7x, 512 devices: a whole 4x4x16 slice. The times are simulated.
512 devices in a mesh: dp: 16 (over y_lo, x, core), mp: 32 (over z, y_hi).
Axes of the slice: x: 4, y: 4 (y_hi: 2, y_lo: 2; y = y_hi * 2 + y_lo), z: 16, core: 2. Of those that a mesh axis runs over, the one named last changes fastest.
Arguments:
- hidden_states: bfloat16 [8192, 2560], P(('dp', 'mp')), may hold values from -60 to 60
- norm_gain: float32 [2560], replicated, may hold values from 0.5 to 1.5
- head_weight: bfloat16 [2560, 65536], P(None, ('dp', 'mp')), may hold values from -64 to 64
- target_ids: int32 [8192], P(('dp', 'mp')), may hold values from 0 to 65535
- response_mask: int32 [8192], P(('dp', 'mp')), may hold values from 0 to 1, as said below
Outputs:
- token_logprob: float32 [8192], P(('dp', 'mp'))
- token_entropy: float32 [8192], P(('dp', 'mp'))
Inputs may be any that keep to these rules, and one draw needn't show every extreme that they name: `response_mask`: each aligned run of 256 positions is one rollout: a prompt of 0s, then one span of 1s, then padding 0s.
All inputs are finite; a program needn't handle non-finite values.
Results may differ from a plain program's by a relative error of at most 0.0048.
Values may be sent and summed in bfloat16 or wider, within the bound.
No kernel may reach another device: no remote copies, remote signals or barrier semaphores. Data moves between devices by JAX's collectives and lax.ppermute only.
A program may use at most 64 MiB of HBM per device.

v0:
```python
import jax
import jax.numpy as jnp
from jax import lax
from jax.sharding import PartitionSpec as P

lowest_start = -1e30


def combined_all(value, axis, join):
    pieces = jax.tree.map(lambda part: lax.all_gather(part, axis), value)
    head = jax.tree.map(lambda part: part[0], pieces)
    tail = jax.tree.map(lambda part: part[1:], pieces)
    total, _ = lax.scan(lambda total, share: (join(total, share), None), head, tail)
    return total


def combine_stats(earlier, later):
    top_first, sum_first, moment_first, chosen_first = earlier
    top_second, sum_second, moment_second, chosen_second = later
    top_new = jnp.maximum(top_first, top_second)
    factor_first = jnp.exp(top_first - top_new)
    factor_second = jnp.exp(top_second - top_new)
    return (
        top_new,
        sum_first * factor_first + sum_second * factor_second,
        moment_first * factor_first + moment_second * factor_second,
        chosen_first + chosen_second,
    )


def start_stats(row_count):
    zeros = jnp.zeros((row_count,), jnp.float32)
    return (jnp.full((row_count,), lowest_start, jnp.float32), zeros, zeros, zeros)


def add_columns(running, token_rows, token_targets, column_piece, column_ids):
    logits = jnp.dot(token_rows, column_piece, preferred_element_type=jnp.float32)
    piece_top = jnp.max(logits, axis=1)
    shifted = jnp.exp(logits - piece_top[:, None])
    target_hit = token_targets[:, None] == column_ids[None, :]
    piece_stats = (
        piece_top,
        jnp.sum(shifted, axis=1),
        jnp.sum(shifted * logits, axis=1),
        jnp.sum(jnp.where(target_hit, logits, 0.0), axis=1),
    )
    return combine_stats(running, piece_stats)


def local(hidden_states, norm_gain, head_weight, target_ids, response_mask):
    states = hidden_states.astype(jnp.float32)
    mean_square = jnp.mean(states * states, axis=1, keepdims=True)
    normed = (states * lax.rsqrt(mean_square + 1e-06) * norm_gain[None, :]).astype(jnp.bfloat16)
    mp_count = lax.axis_size("mp")
    mp_index = lax.axis_index("mp")
    shard_cols = head_weight.shape[1]
    send_count = normed.shape[0]
    group_states, group_targets = (
        lax.all_gather(normed, "mp", axis=0, tiled=True),
        lax.all_gather(target_ids, "mp", axis=0, tiled=True),
    )
    column_piece = lax.all_gather(head_weight, "dp", axis=1, tiled=True)
    positions = jnp.arange(column_piece.shape[1], dtype=jnp.int32)
    owners = positions // shard_cols
    column_ids = (owners * mp_count + mp_index) * shard_cols + positions % shard_cols
    partial_stats = add_columns(
        start_stats(group_states.shape[0]), group_states, group_targets, column_piece, column_ids
    )
    merged = combined_all(partial_stats, "mp", combine_stats)
    first_row = mp_index * send_count
    top_logit, weight_total, moment, chosen = [
        lax.dynamic_slice_in_dim(member, first_row, send_count) for member in merged
    ]
    log_total = top_logit + jnp.log(weight_total)
    logprob = chosen - log_total
    entropy = log_total - moment / weight_total
    scored = response_mask.astype(jnp.float32)
    return (logprob * scored, entropy * scored)


def solution(mesh):
    return jax.shard_map(
        local,
        mesh=mesh,
        in_specs=(
            P(("dp", "mp"), None),
            P(),
            P(None, ("dp", "mp")),
            P(("dp", "mp")),
            P(("dp", "mp")),
        ),
        out_specs=(P(("dp", "mp")), P(("dp", "mp"))),
        check_vma=False,
    )
```

profile of v0, /device:TPU:16, one launch (start us, length us, event | category | flops | bytes accessed | tf_op | source)
XLA Modules:
  0.0 556.4 jit_solution(13439225483847453185)
XLA Ops:
  7.2 0.0 all-gather.8.cloned.1.call-start
  7.2 1.0 fusion.1
  8.2 1.6 fusion.3
  9.9 0.0 all-gather.8.cloned.1.call-update
  9.9 0.0 all-gather.10.cloned.1.call-start
  9.9 0.7 all-gather.10.cloned.1.call-update
  10.6 1.3 dynamic-slice
  12.6 0.9 dynamic-update-slice
  13.4 30.9 %all-reduce = s32[512]{0:T(512)S(1)} all-reduce(s32[512]{0:T(512)S(1)} %dynamic-update-slice), channel_id=1, replica_groups=mesh['dp'=16,'mp'=32] {'mp'}, use_global_device_ids=true, to_apply=%add | all-reduce | flops 512 | bytes 4096
  44.3 121.9 %all-gather.8.cloned.1.call-done = bf16[512,2560]{1,0:T(8,128)(2,1)} async-done(((bf16[16,2560]{1,0:T(8,128)(2,1)}), bf16[512,2560]{1,0:T(8,128)(2,1)}) %all-gather.8.cloned.1.call-update) | async-done | bytes 2621456 | tf_op jit(solution)/shard_map/all_gather | solution.py:59
  166.3 74.4 %all-gather.10.cloned.1.call-done = bf16[2560,2048]{1,0:T(8,128)(2,1)} async-done(((bf16[2560,128]{1,0:T(8,128)(2,1)}), bf16[2560,2048]{1,0:T(8,128)(2,1)}) %all-gather.10.cloned.1.call-update) | async-done | bytes 10485776 | tf_op jit(solution)/shard_map/all_gather | solution.py:62
  240.7 9.2 %fusion.15 = (f32[512]{0:T(512)S(1)}, f32[512,2048]{1,0:T(8,128)S(1)}) fusion(bf16[512,2560]{1,0:T(8,128)(2,1)} %all-gather.8.cloned.1.call-done, bf16[2560,2048]{1,0:T(8,128)(2,1)} %all-gather.10.cloned.1.call-done), kind=kOutput, calls=%fused_computation.45 | convolution fusion | flops 5369757184 | bytes 17303552 | tf_op jit(solution)/shard_map/dot_general | solution.py:37
  249.9 0.0 copy-start
  249.9 1.9 multiply_reduce_fusion
  251.8 73.0 %all-gather.3 = f32[32,1,512]{2,1,0:T(1,128)S(1)} all-gather(f32[1,1,512]{2,1,0:T(1,128)S(1)} %get-tuple-element.85), channel_id=1, replica_groups=mesh['dp'=16,'mp'=32] {'mp'}, dimensions={0}, use_global_device_ids=true | all-gather | bytes 67584 | tf_op jit(solution)/shard_map/all_gather | solution.py:10
  324.8 75.5 %all-gather.1 = f32[32,1,512]{2,1,0:T(1,128)S(1)} all-gather(f32[1,1,512]{2,1,0:T(1,128)S(1)} %get-tuple-element.87), channel_id=1, replica_groups=mesh['dp'=16,'mp'=32] {'mp'}, dimensions={0}, use_global_device_ids=true | all-gather | bytes 67584 | tf_op jit(solution)/shard_map/all_gather | solution.py:10
  400.3 70.7 %all-gather.2 = f32[32,1,512]{2,1,0:T(1,128)S(1)} all-gather(f32[1,1,512]{2,1,0:T(1,128)S(1)} %get-tuple-element.86), channel_id=1, replica_groups=mesh['dp'=16,'mp'=32] {'mp'}, dimensions={0}, use_global_device_ids=true | all-gather | bytes 67584 | tf_op jit(solution)/shard_map/all_gather | solution.py:10
  471.0 74.2 %all-gather.4 = f32[32,1,512]{2,1,0:T(1,128)S(1)} all-gather(f32[1,1,512]{2,1,0:T(1,128)S(1)} %bitcast.54), channel_id=2, replica_groups=mesh['dp'=16,'mp'=32] {'mp'}, dimensions={0}, use_global_device_ids=true | all-gather | bytes 67584 | tf_op jit(solution)/shard_map/all_gather | solution.py:10
  545.3 3.6 while.16
  549.0 0.0 copy-done
  549.0 0.6 subtract_multiply_fusion
  (202 shorter events, 2.3 us)
Async XLA Ops:
  7.2 159.1 %all-gather.8.cloned.1.call-start = ((), (), s32[]{:S(2)}) async-start(), calls=%async_computation | async-start | bytes 2703360 | tf_op jit(solution)/shard_map/all_gather | solution.py:59
  9.9 230.8 %all-gather.10.cloned.1.call-start = ((), (), s32[]{:S(2)}) async-start(), calls=%async_computation.1 | async-start | bytes 11141120 | tf_op jit(solution)/shard_map/all_gather | solution.py:62
  249.9 299.1 %copy-start = (s32[16]{0:T(128)S(1)}, s32[16]{0:T(128)}, u32[]{:S(2)}) copy-start(s32[16]{0:T(128)} %param.11) | copy-start | bytes 196
Sparse Core Ops, SparseCore 0:
  11.1 155.1 all-gather.7
  168.3 72.2 all-gather.9
where the time goes:
time: 557 us; the launch traced here: 556 us
  blocking collectives  324 us (58%)
  waiting for transfers between devices  197 us (35%)
  between operations  14.8 us (3%)
  matrix products  9.23 us (2%)
  other arithmetic  6.51 us (1%)
    all_gather x4, blocking collectives, combined_all(): pieces = jax.tree.map(lambda part: lax.all_gather(part, axis), value)  293 us
    all_gather x1, waiting for transfers between devices, local(): lax.all_gather(normed, 'mp', axis=0, tiled=True)  122 us
    all_gather x1, waiting for transfers between devices, local(): column_piece = lax.all_gather(head_weight, 'dp', axis=1, tiled=True)  74.4 us
    unnamed x1, blocking collectives  30.9 us
  transfers between devices with their start and end apart: 2, of which 2 were waited for; matrix products, arithmetic and copies ran while one was open for 0% of the time, Pallas kernels for 0%

commit v1 on v0

--- a/solution.py
+++ b/solution.py
@@ -4,6 +4,12 @@
 from jax.sharding import PartitionSpec as P
 
 lowest_start = -1e30
+
+
+def set_racks_over_axis(local_x):
+    k_now = jnp.stack([local_x for _ in range(lax.axis_size("dp"))])
+    field_out = lax.all_to_all(k_now, "dp", 0, 0)
+    return jnp.concatenate(field_out, axis=1)
 
 
 def combined_all(value, axis, join):
@@ -59,7 +65,7 @@
         lax.all_gather(normed, "mp", axis=0, tiled=True),
         lax.all_gather(target_ids, "mp", axis=0, tiled=True),
     )
-    column_piece = lax.all_gather(head_weight, "dp", axis=1, tiled=True)
+    column_piece = set_racks_over_axis(head_weight)
     positions = jnp.arange(column_piece.shape[1], dtype=jnp.int32)
     owners = positions // shard_cols
     column_ids = (owners * mp_count + mp_index) * shard_cols + positions % shard_cols

time: 557 us -> 529 us (0.950)
  the two profiles are of different devices: /device:TPU:16 before, /device:TPU:4 now
where the time goes in v1:
time: 529 us
  blocking collectives  385 us (73%)
  waiting for transfers between devices  94.4 us (18%)
  between operations  14.8 us (3%)
  starting transfers between devices  10.6 us (2%)
  matrix products  9.29 us (2%)
  local copies, waits for them, and re-layouts  8.64 us (2%)
    all_gather x4, blocking collectives, combined_all(): pieces = jax.tree.map(lambda part: lax.all_gather(part, axis), value)  290 us
    unnamed x1, blocking collectives  95.1 us
    all_gather x1, waiting for transfers between devices, local(): lax.all_gather(normed, 'mp', axis=0, tiled=True)  94.4 us
  transfers between devices with their start and end apart: 2, of which 1 were waited for; matrix products, arithmetic and copies ran while one was open for 0% of the time, Pallas kernels for 0%

profile of v1, /device:TPU:4, one launch (start us, length us, event | category | flops | bytes accessed | tf_op | source)
XLA Modules:
  0.0 528.8 jit_solution(6415592467981843410)
XLA Ops:
  7.2 1.3 copy.8
  8.5 4.8 stack.2
  13.4 10.6 %all-to-all-start = ((bf16[16,2560,128]{1,2,0:T(8,128)(2,1)}), bf16[16,2560,128]{1,2,0:T(8,128)(2,1)}, u32[]{:S(2)}, u32[]{:S(2)}) async-start(bf16[16,2560,128]{1,2,0:T(8,128)(2,1)} %stack.2), calls=%async_computation | async-start | bytes 20971520 | tf_op jit(solution)/shard_map/all_to_all | solution.py:11
  23.9 0.0 all-gather.7.cloned.1.call-start
  24.0 0.0 copy-done
  24.0 0.1 fusion.1
  24.1 0.0 copy-done.1
  24.1 0.7 fusion.3
  24.8 0.0 all-gather.7.cloned.1.call-update
  24.9 1.3 dynamic-slice
  26.8 0.0 copy-done.3
  26.8 0.2 dynamic-update-slice
  27.1 95.1 %all-reduce = s32[512]{0:T(512)S(1)} all-reduce(s32[512]{0:T(512)S(1)} %dynamic-update-slice), channel_id=1, replica_groups=mesh['dp'=16,'mp'=32] {'mp'}, use_global_device_ids=true, to_apply=%add | all-reduce | flops 512 | bytes 4096
  122.2 94.4 %all-gather.7.cloned.1.call-done = bf16[512,2560]{1,0:T(8,128)(2,1)} async-done(((bf16[16,2560]{1,0:T(8,128)(2,1)}), bf16[512,2560]{1,0:T(8,128)(2,1)}) %all-gather.7.cloned.1.call-update) | async-done | bytes 2621456 | tf_op jit(solution)/shard_map/all_gather | solution.py:65
  216.6 0.0 all-to-all-done
  216.6 9.3 %fusion.15 = (f32[512]{0:T(512)S(1)}, f32[512,2048]{1,0:T(8,128)S(1)}) fusion(bf16[512,2560]{1,0:T(8,128)(2,1)} %all-gather.7.cloned.1.call-done, bf16[2560,2048]{0,1:T(8,128)(2,1)} %bitcast.5), kind=kOutput, calls=%fused_computation.45 | convolution fusion | flops 5369757184 | bytes 17303552 | tf_op jit(solution)/shard_map/dot_general | solution.py:43
  225.9 0.0 copy-start.2
  225.9 1.7 multiply_reduce_fusion
  227.7 72.9 %all-gather.2 = f32[32,1,512]{2,1,0:T(1,128)S(1)} all-gather(f32[1,1,512]{2,1,0:T(1,128)S(1)} %get-tuple-element.86), channel_id=1, replica_groups=mesh['dp'=16,'mp'=32] {'mp'}, dimensions={0}, use_global_device_ids=true | all-gather | bytes 67584 | tf_op jit(solution)/shard_map/all_gather | solution.py:16
  300.6 72.1 %all-gather.3 = f32[32,1,512]{2,1,0:T(1,128)S(1)} all-gather(f32[1,1,512]{2,1,0:T(1,128)S(1)} %get-tuple-element.85), channel_id=1, replica_groups=mesh['dp'=16,'mp'=32] {'mp'}, dimensions={0}, use_global_device_ids=true | all-gather | bytes 67584 | tf_op jit(solution)/shard_map/all_gather | solution.py:16
  372.7 72.9 %all-gather.1 = f32[32,1,512]{2,1,0:T(1,128)S(1)} all-gather(f32[1,1,512]{2,1,0:T(1,128)S(1)} %get-tuple-element.87), channel_id=1, replica_groups=mesh['dp'=16,'mp'=32] {'mp'}, dimensions={0}, use_global_device_ids=true | all-gather | bytes 67584 | tf_op jit(solution)/shard_map/all_gather | solution.py:16
  445.6 72.1 %all-gather.4 = f32[32,1,512]{2,1,0:T(1,128)S(1)} all-gather(f32[1,1,512]{2,1,0:T(1,128)S(1)} %bitcast.57), channel_id=2, replica_groups=mesh['dp'=16,'mp'=32] {'mp'}, dimensions={0}, use_global_device_ids=true | all-gather | bytes 67584 | tf_op jit(solution)/shard_map/all_gather | solution.py:16
  517.7 3.6 while.16
  521.4 0.6 subtract_multiply_fusion
  (206 shorter events, 2.4 us)
Async XLA Ops:
  13.3 10.6 %copy-start = (bf16[16,2560]{1,0:T(8,128)(2,1)S(1)}, bf16[16,2560]{1,0:T(8,128)(2,1)}, u32[]{:S(2)}) copy-start(bf16[16,2560]{1,0:T(8,128)(2,1)} %param.7) | copy-start | bytes 245764
  13.3 10.8 %copy-start.1 = (f32[2560]{0:T(1024)S(1)}, f32[2560]{0:T(1024)}, u32[]{:S(2)}) copy-start(f32[2560]{0:T(1024)} %param.8) | copy-start | bytes 30724
  13.3 13.5 %copy-start.3 = (s32[16]{0:T(128)S(1)}, s32[16]{0:T(128)}, u32[]{:S(2)}) copy-start(s32[16]{0:T(128)} %param.10) | copy-start | bytes 196
  13.4 203.3 %all-to-all-start = ((bf16[16,2560,128]{1,2,0:T(8,128)(2,1)}), bf16[16,2560,128]{1,2,0:T(8,128)(2,1)}, u32[]{:S(2)}, u32[]{:S(2)}) async-start(bf16[16,2560,128]{1,2,0:T(8,128)(2,1)} %stack.2), calls=%async_computation | async-start | bytes 20971520 | tf_op jit(solution)/shard_map/all_to_all | solution.py:11
  23.9 192.7 %all-gather.7.cloned.1.call-start = ((), (), s32[]{:S(2)}) async-start(), calls=%async_computation.1 | async-start | bytes 2703360 | tf_op jit(solution)/shard_map/all_gather | solution.py:65
  225.9 295.4 %copy-start.2 = (s32[16]{0:T(128)S(1)}, s32[16]{0:T(128)}, u32[]{:S(2)}) copy-start(s32[16]{0:T(128)} %param.11) | copy-start | bytes 196
Sparse Core Ops, SparseCore 0:
  27.8 188.7 all-gather.6
